TPU v7x, 32 devices: a whole 2x2x4 slice. The times are simulated.
32 devices in a mesh: row: 8 (over z, y), col: 4 (over x, core).
Axes of the slice: x: 2, y: 2, z: 4, core: 2. Of those that a mesh axis runs over, the one named last changes fastest.
Arguments:
- factor: float32 [4, 8, 256, 1024], P(None, 'row', None, 'col'), may hold values from -0.1875 to 0.1875
- rhs: float32 [4, 8, 256, 4096], P(None, 'row', None, 'col'), may hold values from -6 to 6
- diag_inv: float32 [4, 256, 256], replicated, may hold values from -0.5 to 1.3, as said below
Outputs:
- updated: float32 [4, 8, 256, 4096], P(None, 'row', None, 'col')
Inputs may be any that keep to these rules, and one draw needn't show every extreme that they name: Each diag_inv[k] is lower triangular with its diagonal between 0.7 and 1.3.
All inputs are finite; a program needn't handle non-finite values.
Results may differ from a plain program's by a relative error of at most 0.0001.
Values sent between devices are 32-bit elements; how exact they have to be, the bound alone decides.
No kernel may reach another device: no remote copies, remote signals or barrier semaphores. Data moves between devices by JAX's collectives and lax.ppermute only.
A program may use at most 64 MiB of HBM per device.

v0:
```python
import jax
import jax.numpy as jnp
from jax import lax
from jax.sharding import PartitionSpec as P

STEPS = 4


def broadcast(block, axis, holder):
    block = jnp.where(lax.axis_index(axis) == holder, block, jnp.zeros_like(block))
    return lax.psum(block, axis)


def matmul(left, right):
    return jnp.dot(left, right, precision=lax.Precision.HIGHEST, preferred_element_type=jnp.float32)


def per_device(factor, rhs, diag_inv):
    row_count = lax.axis_size("row")
    block_size = rhs.shape[2]
    local_blocks = rhs.shape[0]
    panel = lax.all_gather(factor, "col", axis=3, tiled=True)
    flat_panel = panel.reshape(local_blocks * block_size, STEPS * block_size)
    position = lax.axis_index("row")
    blocks = (jnp.arange(local_blocks, dtype=jnp.int32) * row_count + position)[:, None, None, None]
    work = rhs
    for step in range(STEPS):
        candidate = matmul(diag_inv[step], work[0, 0])
        solved = broadcast(candidate, "row", step)
        update = matmul(flat_panel[:, step * block_size : (step + 1) * block_size], solved).reshape(
            work.shape
        )
        work = jnp.where(
            blocks > step, work - update, jnp.where(blocks == step, solved[None, None], work)
        )
    return work


def solution(mesh):
    return jax.shard_map(
        per_device,
        mesh=mesh,
        in_specs=(P(None, "row", None, "col"), P(None, "row", None, "col"), P()),
        out_specs=P(None, "row", None, "col"),
        check_vma=False,
    )
```

profile of v0, /device:TPU:0, one launch (start us, length us, event | category | flops | bytes accessed | tf_op | source)
XLA Modules:
  0.0 394.6 jit_solution(5680344564141285933)
XLA Ops:
  7.4 3.3 convolution_select_fusion.3
  10.7 0.0 all-reduce.5.cloned.1.call-update
  10.7 0.0 all-gather.2.cloned.1.call-start
  10.8 0.5 all-gather.2.cloned.1.call-update
  11.3 0.0 all-reduce.7.cloned.1.call-start
  11.4 81.4 %all-reduce.5.cloned.1.call-done = f32[256,1024]{1,0:T(8,128)} async-done(((f32[256,1024]{1,0:T(8,128)}), f32[256,1024]{1,0:T(8,128)}) %all-reduce.5.cloned.1.call-update) | async-done | bytes 1048592 | tf_op jit(solution)/shard_map/psum | solution.py:11
  92.7 5.4 %fusion.9 = f32[1024,1024]{0,1:T(8,128)S(1)} fusion(f32[256,1024]{1,0:T(8,128)} %all-reduce.5.cloned.1.call-done, f32[1024,1024]{1,0:T(8,128)} %bitcast.59), kind=kOutput, calls=%fused_computation.20 | convolution fusion | flops 3221225472 | bytes 6291456 | tf_op jit(solution)/shard_map/dot_general | solution.py:15
  98.2 0.0 copy-start.8
  98.2 1.6 select_select_fusion.3
  99.8 2.0 copy-done.1
  101.8 2.8 fusion.2
  104.7 0.0 all-reduce.7.cloned.1.call-update
  104.7 0.2 all-reduce.9.cloned.1.call-start
  104.9 77.8 %all-reduce.7.cloned.1.call-done = f32[256,1024]{0,1:T(8,128)} async-done(((f32[256,1024]{0,1:T(8,128)}), f32[256,1024]{0,1:T(8,128)}) %all-reduce.7.cloned.1.call-update) | async-done | bytes 1048592 | tf_op jit(solution)/shard_map/psum | solution.py:11
  182.7 7.1 %fusion.7 = f32[1024,1024]{0,1:T(8,128)} fusion(f32[256,1024]{0,1:T(8,128)} %all-reduce.7.cloned.1.call-done, f32[1024,1024]{1,0:T(8,128)} %bitcast.60), kind=kOutput, calls=%fused_computation.17 | convolution fusion | flops 3221225472 | bytes 6291456 | tf_op jit(solution)/shard_map/dot_general | solution.py:15
  189.8 0.3 copy.6
  190.2 4.7 %select_select_fusion.2 = f32[4,1,256,1024]{3,2,1,0:T(8,128)S(1)} fusion(f32[4,1,256,1024]{3,2,1,0:T(8,128)} %copy-done.1, f32[4,1,256,1024]{3,2,1,0:T(8,128)} %bitcast.56, f32[256,1024]{1,0:T(8,128)S(1)} %copy.6, pred[4]{0:T(512)(128)(4,1)S(1)} %get-tuple-element.7, pred[4]{0:T(512)(128)(4,1)S(1)} %get-tuple-element.8), kind=kLoop, calls=%fused_computation.2 | loop fusion | flops 3145728 | bytes 13631496 | tf_op jit(solution)/shard_map/jit(_where)/select_n | solution.py:33
  194.9 2.0 copy-done
  196.9 2.8 fusion.1
  199.8 0.0 all-reduce.9.cloned.1.call-update
  199.8 0.3 all-reduce.11.cloned.1.call-start
  200.1 77.8 %all-reduce.9.cloned.1.call-done = f32[256,1024]{0,1:T(8,128)} async-done(((f32[256,1024]{0,1:T(8,128)}), f32[256,1024]{0,1:T(8,128)}) %all-reduce.9.cloned.1.call-update) | async-done | bytes 1048592 | tf_op jit(solution)/shard_map/psum | solution.py:11
  277.9 7.1 %fusion.5 = f32[1024,1024]{0,1:T(8,128)} fusion(f32[256,1024]{0,1:T(8,128)} %all-reduce.9.cloned.1.call-done, f32[1024,1024]{1,0:T(8,128)} %bitcast.61), kind=kOutput, calls=%fused_computation.14 | convolution fusion | flops 3221225472 | bytes 6291456 | tf_op jit(solution)/shard_map/dot_general | solution.py:15
  285.0 0.3 copy.8
  285.4 4.7 %select_select_fusion.1 = f32[4,1,256,1024]{3,2,1,0:T(8,128)S(1)} fusion(f32[4,1,256,1024]{3,2,1,0:T(8,128)} %copy-done, f32[4,1,256,1024]{3,2,1,0:T(8,128)} %bitcast.57, f32[256,1024]{1,0:T(8,128)S(1)} %copy.8, pred[4]{0:T(512)(128)(4,1)S(1)} %get-tuple-element.9, pred[4]{0:T(512)(128)(4,1)S(1)} %get-tuple-element.10), kind=kLoop, calls=%fused_computation.1 | loop fusion | flops 3145728 | bytes 13631496 | tf_op jit(solution)/shard_map/jit(_where)/select_n | solution.py:33
  290.1 2.0 copy-done.2
  292.1 2.8 fusion
  295.0 0.0 all-reduce.11.cloned.1.call-update
  295.0 78.0 %all-reduce.11.cloned.1.call-done = f32[256,1024]{0,1:T(8,128)} async-done(((f32[256,1024]{0,1:T(8,128)}), f32[256,1024]{0,1:T(8,128)}) %all-reduce.11.cloned.1.call-update) | async-done | bytes 1048592 | tf_op jit(solution)/shard_map/psum | solution.py:11
  373.0 7.1 %fusion.3 = f32[1024,1024]{0,1:T(8,128)} fusion(f32[256,1024]{0,1:T(8,128)} %all-reduce.11.cloned.1.call-done, f32[1024,1024]{1,0:T(8,128)} %bitcast.62), kind=kOutput, calls=%fused_computation.11 | convolution fusion | flops 3221225472 | bytes 6291456 | tf_op jit(solution)/shard_map/dot_general | solution.py:15
  380.1 0.3 copy.10
  380.4 7.1 %select_select_fusion = f32[4,1,256,1024]{3,2,1,0:T(8,128)} fusion(f32[4,1,256,1024]{3,2,1,0:T(8,128)} %copy-done.2, f32[4,1,256,1024]{3,2,1,0:T(8,128)} %bitcast.55, f32[256,1024]{1,0:T(8,128)S(1)} %copy.10, pred[4]{0:T(512)(128)(4,1)S(1)} %get-tuple-element.11, pred[4]{0:T(512)(128)(4,1)S(1)} %get-tuple-element.12), kind=kLoop, calls=%fused_computation | loop fusion | flops 3145728 | bytes 13631496 | tf_op jit(solution)/shard_map/jit(_where)/select_n | solution.py:33
  (20 shorter events, 0.1 us)
Async XLA Ops:
  7.4 85.4 %all-reduce.5.cloned.1.call-start = ((), (), s32[]{:S(2)}) async-start(), calls=%async_computation | async-start | bytes 2097152 | tf_op jit(solution)/shard_map/psum | solution.py:11
  10.7 82.0 %all-gather.2.cloned.1.call-start = ((), (), s32[]{:S(2)}) async-start(), calls=%async_computation.1 | async-start | bytes 5242880 | tf_op jit(solution)/shard_map/all_gather | solution.py:22
  11.3 171.4 %all-reduce.7.cloned.1.call-start = ((), (), s32[]{:S(2)}) async-start(), calls=%async_computation.2 | async-start | bytes 2097152 | tf_op jit(solution)/shard_map/psum | solution.py:11
  92.7 5.4 %copy-start.7 = (f32[256,1024]{1,0:T(8,128)S(1)}, f32[256,1024]{1,0:T(8,128)}, u32[]{:S(2)}) copy-start(f32[256,1024]{1,0:T(8,128)} %all-reduce.5.cloned.1.call-done) | copy-start | bytes 3145732
  92.7 5.4 %copy-start.3 = (f32[4,1,256,1024]{3,2,1,0:T(8,128)S(1)}, f32[4,1,256,1024]{3,2,1,0:T(8,128)}, u32[]{:S(2)}) copy-start(f32[4,1,256,1024]{3,2,1,0:T(8,128)} %param.4) | copy-start | bytes 12582916
  98.2 3.7 copy-start.8
  99.8 2.0 copy-start.1
  104.7 173.2 %all-reduce.9.cloned.1.call-start = ((), (), s32[]{:S(2)}) async-start(), calls=%async_computation.3 | async-start | bytes 2097152 | tf_op jit(solution)/shard_map/psum | solution.py:11
  182.7 7.1 %copy-start.4 = (f32[256,1024]{0,1:T(8,128)S(1)}, f32[256,1024]{0,1:T(8,128)}, u32[]{:S(2)}) copy-start(f32[256,1024]{0,1:T(8,128)} %all-reduce.7.cloned.1.call-done) | copy-start | bytes 3145732
  194.9 2.0 copy-start
  199.8 173.2 %all-reduce.11.cloned.1.call-start = ((), (), s32[]{:S(2)}) async-start(), calls=%async_computation.4 | async-start | bytes 2097152 | tf_op jit(solution)/shard_map/psum | solution.py:11
  277.9 7.1 %copy-start.5 = (f32[256,1024]{0,1:T(8,128)S(1)}, f32[256,1024]{0,1:T(8,128)}, u32[]{:S(2)}) copy-start(f32[256,1024]{0,1:T(8,128)} %all-reduce.9.cloned.1.call-done) | copy-start | bytes 3145732
  290.1 2.0 copy-start.2
  373.0 7.1 %copy-start.6 = (f32[256,1024]{0,1:T(8,128)S(1)}, f32[256,1024]{0,1:T(8,128)}, u32[]{:S(2)}) copy-start(f32[256,1024]{0,1:T(8,128)} %all-reduce.11.cloned.1.call-done) | copy-start | bytes 3145732
Sparse Core Ops, SparseCore 0:
  11.7 81.0 all-reduce.4
  104.8 77.8 all-reduce.6
  199.9 77.9 all-reduce.8
  295.1 77.8 all-reduce.10
Sparse Core Ops, SparseCore 1:
  12.8 37.0 all-gather.1
where the time goes:
time: 395 us
  waiting for transfers between devices  316 us (80%)
  matrix products  38.6 us (10%)
  other arithmetic  18.2 us (5%)
  between operations  14.7 us (4%)
  local copies, waits for them, and re-layouts  7.04 us (2%)
    psum x4, waiting for transfers between devices, broadcast(): return lax.psum(block, axis)  315 us
    dot_general x8, matrix products, matmul(): jnp.dot(left, right, precision=lax.Precision.HIGHEST, preferred_element_t...  38.6 us
    select_n x4, other arithmetic, per_device(): jnp.where(blocks > step, work - update, jnp.where(blocks == step, solved[...  18.1 us
  transfers between devices with their start and end apart: 5, of which 4 were waited for; matrix products, arithmetic and copies ran while one was open for 0% of the time, Pallas kernels for 0%

commit v1 on v0

--- a/solution.py
+++ b/solution.py
@@ -8,7 +8,7 @@
 
 def broadcast(block, axis, holder):
     block = jnp.where(lax.axis_index(axis) == holder, block, jnp.zeros_like(block))
-    return lax.psum(block, axis)
+    return jnp.sum(lax.all_gather(block, axis_name=axis), 0)
 
 
 def matmul(left, right):

time: 395 us -> 645 us (1.63)
  waiting for transfers between devices: 316 us -> 528 us
  local copies, waits for them, and re-layouts: 7.04 us -> 29.5 us
  other arithmetic: 18.2 us -> 30.3 us
    all_gather x0 -> x4, waiting for transfers between devices: none -> 498 us  [broadcast(): return jnp.sum(lax.all_gather(block, axis_name=axis), 0)]
    psum x4 -> x0, waiting for transfers between devices: 315 us -> none  [broadcast(): return lax.psum(block, axis)]
    all_gather x1, waiting for transfers between devices: 0.01 us -> 29.8 us  [per_device(): panel = lax.all_gather(factor, 'col', axis=3, tiled=True)]
    unnamed x18 -> x13, local copies, waits for them, and re-layouts: 6.05 us -> 28.5 us
    reduce_sum x0 -> x4, other arithmetic: none -> 12.2 us  [broadcast(): return jnp.sum(lax.all_gather(block, axis_name=axis), 0)]
  transfers between devices with their start and end apart: 5 -> 5, of which waited for: 4 -> 5; matrix products, arithmetic and copies ran while one was open for 0% -> 1% of each run, Pallas kernels for 0% -> 0%
where the time goes in v1:
time: 645 us; the launch traced here: 638 us
  waiting for transfers between devices  528 us (82%)
  matrix products  36.1 us (6%)
  other arithmetic  30.3 us (5%)
  local copies, waits for them, and re-layouts  29.5 us (5%)
  between operations  13.8 us (2%)
    all_gather x4, waiting for transfers between devices, broadcast(): return jnp.sum(lax.all_gather(block, axis_name=axis), 0)  498 us
    dot_general x8, matrix products, matmul(): jnp.dot(left, right, precision=lax.Precision.HIGHEST, preferred_element_t...  36.1 us
    all_gather x1, waiting for transfers between devices, per_device(): panel = lax.all_gather(factor, 'col', axis=3, tiled=True)  29.8 us
    unnamed x13, local copies, waits for them, and re-layouts  28.5 us
    select_n x4, other arithmetic, per_device(): jnp.where(blocks > step, work - update, jnp.where(blocks == step, solved[...  18.1 us
  transfers between devices with their start and end apart: 5, of which 5 were waited for; matrix products, arithmetic and copies ran while one was open for 1% of the time, Pallas kernels for 0%

profile of v1, /device:TPU:0, one launch (start us, length us, event | category | flops | bytes accessed | tf_op | source)
XLA Modules:
  0.0 638.5 jit_solution(5260800671304562443)
XLA Ops:
  6.5 3.3 convolution_select_fusion.3
  9.9 0.7 all-gather.10.cloned.1.call-update
  10.7 126.5 %all-gather.12.cloned.1.call-done = f32[2048,1024]{1,0:T(8,128)} async-done(((f32[256,1024]{1,0:T(8,128)}), f32[2048,1024]{1,0:T(8,128)}) %all-gather.12.cloned.1.call-update) | async-done | bytes 8388624 | tf_op jit(solution)/shard_map/all_gather | solution.py:11
  137.2 4.4 reduce_sum.36
  141.6 29.8 %all-gather.10.cloned.1.call-done = f32[4,1,256,1024]{3,2,1,0:T(8,128)} async-done(((f32[4,1,256,256]{3,2,1,0:T(8,128)}), f32[4,1,256,1024]{3,2,1,0:T(8,128)}) %all-gather.10.cloned.1.call-update) | async-done | bytes 4194320 | tf_op jit(solution)/shard_map/all_gather | solution.py:22
  171.5 5.1 fusion.9
  176.6 1.6 select_select_fusion.3
  178.2 2.0 copy-done.1
  180.2 2.9 fusion.2
  183.4 124.9 %all-gather.14.cloned.1.call-done = f32[2048,1024]{0,1:T(8,128)} async-done(((f32[256,1024]{0,1:T(8,128)}), f32[2048,1024]{0,1:T(8,128)}) %all-gather.14.cloned.1.call-update) | async-done | bytes 8388624 | tf_op jit(solution)/shard_map/all_gather | solution.py:11
  308.2 7.5 %copy.15 = f32[128,8,8,256]{3,2,1,0:T(8,128)S(1)} copy(f32[128,8,8,256]{3,1,2,0:T(8,128)} %bitcast.76) | data formatting | bytes 16777216
  315.7 2.5 bitcast_reduce_fusion.2
  318.3 6.3 fusion.7
  324.6 0.3 copy.10
  324.9 4.7 select_select_fusion.2
  329.6 2.0 copy-done
  331.7 2.9 fusion.1
  334.6 0.3 all-gather.18.cloned.1.call-start
  334.9 123.0 %all-gather.16.cloned.1.call-done = f32[2048,1024]{0,1:T(8,128)} async-done(((f32[256,1024]{0,1:T(8,128)}), f32[2048,1024]{0,1:T(8,128)}) %all-gather.16.cloned.1.call-update) | async-done | bytes 8388624 | tf_op jit(solution)/shard_map/all_gather | solution.py:11
  457.9 7.5 %copy.16 = f32[128,8,8,256]{3,2,1,0:T(8,128)S(1)} copy(f32[128,8,8,256]{3,1,2,0:T(8,128)} %bitcast.77) | data formatting | bytes 16777216
  465.4 2.5 bitcast_reduce_fusion.1
  467.9 6.3 fusion.5
  474.2 0.3 copy.12
  474.5 4.7 select_select_fusion.1
  479.3 2.0 copy-done.2
  481.3 2.9 fusion
  484.2 123.3 %all-gather.18.cloned.1.call-done = f32[2048,1024]{0,1:T(8,128)} async-done(((f32[256,1024]{0,1:T(8,128)}), f32[2048,1024]{0,1:T(8,128)}) %all-gather.18.cloned.1.call-update) | async-done | bytes 8388624 | tf_op jit(solution)/shard_map/all_gather | solution.py:11
  607.5 7.5 %copy.17 = f32[128,8,8,256]{3,2,1,0:T(8,128)S(1)} copy(f32[128,8,8,256]{3,1,2,0:T(8,128)} %bitcast.78) | data formatting | bytes 16777216
  615.0 2.8 bitcast_reduce_fusion
  617.8 6.3 fusion.3
  624.1 0.3 copy.14
  624.4 7.1 %select_select_fusion = f32[4,1,256,1024]{3,2,1,0:T(8,128)} fusion(f32[4,1,256,1024]{3,2,1,0:T(8,128)} %copy-done.2, f32[4,1,256,1024]{3,2,1,0:T(8,128)} %bitcast.71, f32[256,1024]{1,0:T(8,128)S(1)} %copy.14, pred[4]{0:T(512)(128)(4,1)S(1)} %get-tuple-element.11, pred[4]{0:T(512)(128)(4,1)S(1)} %get-tuple-element.12), kind=kLoop, calls=%fused_computation.3 | loop fusion | flops 3145728 | bytes 13631496 | tf_op jit(solution)/shard_map/jit(_where)/select_n | solution.py:33
  (19 shorter events, 0.4 us)
Async XLA Ops:
  6.5 130.7 %all-gather.12.cloned.1.call-start = ((), (), s32[]{:S(2)}) async-start(), calls=%async_computation.1 | async-start | bytes 9437184 | tf_op jit(solution)/shard_map/all_gather | solution.py:11
  9.9 161.6 %all-gather.10.cloned.1.call-start = ((), (), s32[]{:S(2)}) async-start(), calls=%async_computation | async-start | bytes 5242880 | tf_op jit(solution)/shard_map/all_gather | solution.py:22
  10.6 297.6 %all-gather.14.cloned.1.call-start = ((), (), s32[]{:S(2)}) async-start(), calls=%async_computation.2 | async-start | bytes 9437184 | tf_op jit(solution)/shard_map/all_gather | solution.py:11
  171.5 5.1 copy-start.3
  176.5 3.7 copy-start.4
  178.2 2.0 copy-start.1
  183.2 274.7 %all-gather.16.cloned.1.call-start = ((), (), s32[]{:S(2)}) async-start(), calls=%async_computation.3 | async-start | bytes 9437184 | tf_op jit(solution)/shard_map/all_gather | solution.py:11
  329.6 2.0 copy-start
  334.6 272.9 %all-gather.18.cloned.1.call-start = ((), (), s32[]{:S(2)}) async-start(), calls=%async_computation.4 | async-start | bytes 9437184 | tf_op jit(solution)/shard_map/all_gather | solution.py:11
  479.3 2.0 copy-start.2
Sparse Core Ops, SparseCore 0:
  10.0 127.1 all-gather.11
  138.8 32.6 all-gather.9
  183.3 124.9 all-gather.13
  334.7 123.1 all-gather.15
  484.3 123.1 all-gather.17
